TPU v7x, 256 devices: a whole 4x4x8 slice. The times are simulated.
256 devices in a mesh: row: 16 (over z_lo, x, core), col: 16 (over z_hi, y).
Axes of the slice: x: 4, y: 4, z: 8 (z_hi: 4, z_lo: 2; z = z_hi * 2 + z_lo), core: 2. Of those that a mesh axis runs over, the one named last changes fastest.
Arguments:
- features: bfloat16 [65536, 512], P(('col', 'row')), may hold values from -6 to 6
- weight: bfloat16 [512, 512], replicated, may hold values from -0.25 to 0.25
- entry_values: bfloat16 [16, 16, 32, 128, 128], P('row', 'col'), may hold values from 0.0009994507 to 0.019897461
- block_rows: int32 [16, 16, 32], P('row', 'col'), may hold values from 0 to 31
- block_cols: int32 [16, 16, 32], P('row', 'col'), may hold values from 0 to 31
- entry_counts: int32 [16, 16], P('row', 'col'), may hold values from 8 to 32, as said below
- cotangent: bfloat16 [65536, 512], P(('row', 'col')), may hold values from -1.5 to 1.5
Outputs:
- output: bfloat16 [65536, 512], P(('row', 'col'))
- grad_features: bfloat16 [65536, 512], P(('col', 'row'))
- grad_weight: float32 [512, 512], replicated
Inputs may be any that keep to these rules, and one draw needn't show every extreme that they name: `entry_counts`: each grid cell has at least 8 live slots; at least one cell has all 32 live.
All inputs are finite; a program needn't handle non-finite values.
Results may differ from a plain program's by a relative error of at most 0.022.
Values may be sent and summed in bfloat16 or wider, within the bound.
No kernel may reach another device: no remote copies, remote signals or barrier semaphores. Data moves between devices by JAX's collectives and lax.ppermute only.
A program may use at most 128 MiB of HBM per device.

v0:
```python
import jax
import jax.numpy as jnp
from jax import lax
from jax.sharding import PartitionSpec as P


def block_terms(values, source_ids, target_ids, live_count, source, target_blocks, transpose):
    entry_total = values.shape[0]
    block_side = values.shape[1]
    feature_count = source.shape[1]
    group_size = min(32, entry_total)
    source_tiles = source.reshape(-1, block_side, feature_count)

    def one_group(group_index, running):
        first_entry = group_index * group_size
        tiles = jnp.take(source_tiles, source_ids, axis=0)
        if transpose:
            products = jnp.einsum("kba,kbf->kaf", values, tiles, preferred_element_type=jnp.float32)
        else:
            products = jnp.einsum("kab,kbf->kaf", values, tiles, preferred_element_type=jnp.float32)
        alive_mask = (first_entry + jnp.arange(group_size) < live_count).astype(jnp.float32)
        return running.at[target_ids].add(products * alive_mask[:, None, None])

    zero_sum = jnp.zeros((target_blocks, block_side, feature_count), jnp.float32)
    trip_count = entry_total // group_size
    running = lax.fori_loop(0, trip_count, one_group, zero_sum)
    return running.reshape(target_blocks * block_side, feature_count)


def silu_slope(summed):
    sigmoid_value = jax.nn.sigmoid(summed)
    return sigmoid_value * (1.0 + summed * (1.0 - sigmoid_value))


def shards(features, weight, entry_values, block_rows, block_cols, entry_counts, cotangent):
    values = entry_values[0, 0]
    row_ids = block_rows[0, 0]
    col_ids = block_cols[0, 0]
    live_count = entry_counts[0, 0]
    local_rows = features.shape[0]
    block_side = values.shape[1]
    row_span = lax.axis_size("col") * local_rows
    col_span = lax.axis_size("row") * local_rows
    projected = jnp.dot(features, weight, preferred_element_type=jnp.float32).astype(jnp.bfloat16)
    panel = lax.all_gather(projected, "row", axis=0, tiled=True)
    forward_terms = block_terms(
        values, col_ids, row_ids, live_count, panel, row_span // block_side, False
    )
    own_sum = lax.psum_scatter(
        forward_terms.astype(jnp.bfloat16), "col", scatter_dimension=0, tiled=True
    ).astype(jnp.float32)
    output = jax.nn.silu(own_sum).astype(jnp.bfloat16)
    own_upstream = (cotangent.astype(jnp.float32) * silu_slope(own_sum)).astype(jnp.bfloat16)
    upstream = lax.all_gather(own_upstream, "col", axis=0, tiled=True)
    backward_terms = block_terms(
        values, row_ids, col_ids, live_count, upstream, col_span // block_side, True
    )
    grad_projected = lax.psum_scatter(
        backward_terms.astype(jnp.bfloat16), "row", scatter_dimension=0, tiled=True
    )
    weight_term = lax.dot_general(
        features, grad_projected, (((0,), (0,)), ((), ())), preferred_element_type=jnp.float32
    )
    weight_part = lax.psum_scatter(weight_term, "row", scatter_dimension=0, tiled=True)
    weight_part = lax.psum(weight_part, "col")
    grad_weight = lax.all_gather(weight_part, "row", axis=0, tiled=True)
    grad_features = lax.dot_general(
        grad_projected, weight, (((1,), (1,)), ((), ())), preferred_element_type=jnp.float32
    ).astype(jnp.bfloat16)
    return (output, grad_features, grad_weight)


def solution(mesh):
    placed = (
        P(("col", "row"), None),
        P(),
        P("row", "col", None, None, None),
        P("row", "col", None),
        P("row", "col", None),
        P("row", "col"),
        P(("row", "col"), None),
    )
    return jax.shard_map(
        shards,
        mesh=mesh,
        in_specs=placed,
        out_specs=(P(("row", "col"), None), P(("col", "row"), None), P()),
        check_vma=False,
    )
```

profile of v0, /device:TPU:1, one launch (start us, length us, event | category | flops | bytes accessed | tf_op | source)
XLA Modules:
  0.0 675.2 jit_solution(13709387366234247826)
XLA Ops:
  7.2 2.2 convolution_convert_fusion.1
  12.1 42.2 %all-gather.4.cloned.1.call-done = bf16[4096,512]{1,0:T(8,128)(2,1)} async-done(((bf16[256,512]{1,0:T(8,128)(2,1)}), bf16[4096,512]{1,0:T(8,128)(2,1)}) %all-gather.4.cloned.1.call-update) | async-done | bytes 4194320 | tf_op jit(solution)/shard_map/all_gather | solution.py:45
  54.4 4.9 gather_fusion
  59.3 7.1 %multiply_bitcast_fusion.1 = f32[32,128,512]{1,2,0:T(8,128)} fusion(f32[32]{0:T(128)S(1)} %get-tuple-element.53, bf16[32,128,512]{2,1,0:T(8,128)(2,1)} %gather_fusion, pred[32]{0:T(512)(128)(4,1)S(1)} %get-tuple-element.52, bf16[1,1,32,128,128]{4,3,2,1,0:T(8,128)(2,1)S(1)} %copy-done), kind=kOutput, calls=%fused_computation.5 | convolution fusion | flops 541065216 | bytes 13631648 | tf_op jit(solution)/shard_map/while/body/eval_jaxpr/kab,kbf->kaf/dot_general | solution.py:20
  66.5 9.0 %copy.19 = f32[32,128,512]{2,1,0:T(8,128)} copy(f32[32,128,512]{1,2,0:T(8,128)} %multiply_bitcast_fusion.1) | data formatting | bytes 16777216 | tf_op jit(solution)/shard_map/while/body/eval_jaxpr/mul | solution.py:22
  75.5 4.3 broadcast.55.clone
  79.8 18.5 %scatter_fusion = f32[32,128,512]{2,1,0:T(8,128)} fusion(f32[32,128,512]{2,1,0:T(8,128)} %broadcast.55.clone, s32[32]{0:T(128)S(1)} %fusion.22, f32[32,128,512]{2,1,0:T(8,128)} %copy.19), kind=kCustom, calls=%fused_computation.2 | custom fusion | flops 2097152 | bytes 25165952 | tf_op jit(solution)/shard_map/while/body/eval_jaxpr/scatter-add | solution.py:22
  98.3 6.0 convert_element_type.42
  104.3 95.2 %reduce-scatter.6.cloned.1.call-done = bf16[256,512]{1,0:T(8,128)(2,1)} async-done(((bf16[4096,512]{1,0:T(8,128)(2,1)}), bf16[256,512]{1,0:T(8,128)(2,1)}) %reduce-scatter.6.cloned.1.call-update) | async-done | bytes 262160 | tf_op jit(solution)/shard_map/reduce_scatter | solution.py:49
  199.5 2.0 fusion.21
  201.6 74.7 %all-gather.6.cloned.1.call-done = bf16[4096,512]{1,0:T(8,128)(2,1)} async-done(((bf16[256,512]{1,0:T(8,128)(2,1)}), bf16[4096,512]{1,0:T(8,128)(2,1)}) %all-gather.6.cloned.1.call-update) | async-done | bytes 4194320 | tf_op jit(solution)/shard_map/all_gather | solution.py:54
  276.3 4.9 gather_fusion.1
  281.2 7.1 %multiply_bitcast_fusion = f32[32,128,512]{1,2,0:T(8,128)} fusion(f32[32]{0:T(128)S(1)} %get-tuple-element.53, bf16[32,128,512]{2,1,0:T(8,128)(2,1)} %gather_fusion.1, pred[32]{0:T(512)(128)(4,1)S(1)} %compare_and_fusion, bf16[1,1,32,128,128]{4,3,2,1,0:T(8,128)(2,1)S(1)} %copy-done), kind=kOutput, calls=%fused_computation.4 | convolution fusion | flops 541065216 | bytes 13631648 | tf_op jit(solution)/shard_map/while/body/eval_jaxpr/kba,kbf->kaf/dot_general | solution.py:18
  288.4 9.0 %copy.21 = f32[32,128,512]{2,1,0:T(8,128)} copy(f32[32,128,512]{1,2,0:T(8,128)} %multiply_bitcast_fusion) | data formatting | bytes 16777216 | tf_op jit(solution)/shard_map/while/body/eval_jaxpr/mul | solution.py:22
  297.4 4.3 broadcast.55
  301.7 18.9 %scatter_fusion.1 = f32[32,128,512]{2,1,0:T(8,128)} fusion(f32[32,128,512]{2,1,0:T(8,128)} %broadcast.55, s32[32]{0:T(128)S(1)} %fusion.23, f32[32,128,512]{2,1,0:T(8,128)} %copy.21), kind=kCustom, calls=%fused_computation.3 | custom fusion | flops 2097152 | bytes 25165952 | tf_op jit(solution)/shard_map/while/body/eval_jaxpr/scatter-add | solution.py:22
  320.6 6.0 convert_element_type.48
  326.7 67.3 %reduce-scatter.8.cloned.1.call-done = bf16[256,512]{1,0:T(8,128)(2,1)} async-done(((bf16[4096,512]{1,0:T(8,128)(2,1)}), bf16[256,512]{1,0:T(8,128)(2,1)}) %reduce-scatter.8.cloned.1.call-update) | async-done | bytes 262160 | tf_op jit(solution)/shard_map/reduce_scatter | solution.py:58
  396.7 63.2 %reduce-scatter.10.cloned.1.call-done = f32[32,512]{1,0:T(8,128)} async-done(((f32[512,512]{1,0:T(8,128)}), f32[32,512]{1,0:T(8,128)}) %reduce-scatter.10.cloned.1.call-update) | async-done | bytes 65552
  459.9 1.7 copy.26
  461.7 157.9 %all-reduce.2.cloned.1.call-done = f32[32,512]{0,1:T(8,128)} async-done(((f32[32,512]{0,1:T(8,128)}), f32[32,512]{0,1:T(8,128)}) %all-reduce.2.cloned.1.call-update) | async-done | bytes 65552 | tf_op jit(solution)/shard_map/psum | solution.py:65
  619.6 1.7 copy.22
  622.4 43.7 %all-gather.8.cloned.1.call-done = f32[512,512]{1,0:T(8,128)} async-done(((f32[32,512]{1,0:T(8,128)}), f32[512,512]{1,0:T(8,128)}) %all-gather.8.cloned.1.call-update) | async-done | bytes 1048592 | tf_op jit(solution)/shard_map/all_gather | solution.py:66
  666.1 2.3 copy.32
  (41 shorter events, 6.1 us)
Async XLA Ops:
  7.2 52.2 %copy-start = (bf16[1,1,32,128,128]{4,3,2,1,0:T(8,128)(2,1)S(1)}, bf16[1,1,32,128,128]{4,3,2,1,0:T(8,128)(2,1)}, u32[]{:S(2)}) copy-start(bf16[1,1,32,128,128]{4,3,2,1,0:T(8,128)(2,1)} %param.11) | copy-start | bytes 3145732
  7.2 47.2 %all-gather.4.cloned.1.call-start = ((), (), s32[]{:S(2)}) async-start(), calls=%async_computation.3 | async-start | bytes 4456448 | tf_op jit(solution)/shard_map/all_gather | solution.py:45
  9.5 190.0 %reduce-scatter.6.cloned.1.call-start = ((), (), s32[]{:S(2)}) async-start(), calls=%async_computation.4 | async-start | bytes 4456448 | tf_op jit(solution)/shard_map/reduce_scatter | solution.py:49
  104.2 95.2 %copy-start.5 = (bf16[256,512]{1,0:T(8,128)(2,1)S(1)}, bf16[256,512]{1,0:T(8,128)(2,1)}, u32[]{:S(2)}) copy-start(bf16[256,512]{1,0:T(8,128)(2,1)} %param.15) | copy-start | bytes 786436
  104.3 97.3 %copy-start.7 = (s32[1,1,32]{2,1,0:T(1,128)S(1)}, s32[1,1,32]{2,1,0:T(1,128)}, u32[]{:S(2)}) copy-start(s32[1,1,32]{2,1,0:T(1,128)} %param.12) | copy-start | bytes 388
  104.3 97.3 %copy-start.6 = (s32[1,1,32]{2,1,0:T(1,128)S(1)}, s32[1,1,32]{2,1,0:T(1,128)}, u32[]{:S(2)}) copy-start(s32[1,1,32]{2,1,0:T(1,128)} %param.13) | copy-start | bytes 388
  104.3 172.0 %all-gather.6.cloned.1.call-start = ((), (), s32[]{:S(2)}) async-start(), calls=%async_computation.5 | async-start | bytes 4456448 | tf_op jit(solution)/shard_map/all_gather | solution.py:54
  201.5 192.5 %reduce-scatter.8.cloned.1.call-start = ((), (), s32[]{:S(2)}) async-start(), calls=%async_computation.6 | async-start | bytes 4456448 | tf_op jit(solution)/shard_map/reduce_scatter | solution.py:58
  326.6 67.4 %copy-start.3 = (bf16[256,512]{1,0:T(8,128)(2,1)S(1)}, bf16[256,512]{1,0:T(8,128)(2,1)}, u32[]{:S(2)}) copy-start(bf16[256,512]{1,0:T(8,128)(2,1)} %param.9) | copy-start | bytes 786436
  326.6 294.7 %copy-start.2 = (bf16[512,512]{1,0:T(8,128)(2,1)S(1)}, bf16[512,512]{1,0:T(8,128)(2,1)}, u32[]{:S(2)}) copy-start(bf16[512,512]{1,0:T(8,128)(2,1)} %param.10) | copy-start | bytes 1572868
  326.6 341.8 %copy-start.1 = (bf16[1,1,32,128,128]{4,3,2,1,0:T(8,128)(2,1)S(1)}, bf16[1,1,32,128,128]{4,3,2,1,0:T(8,128)(2,1)}, u32[]{:S(2)}) copy-start(bf16[1,1,32,128,128]{4,3,2,1,0:T(8,128)(2,1)} %param.11) | copy-start | bytes 3145732
  326.6 133.3 %reduce-scatter.10.cloned.1.call-start = ((), (), s32[]{:S(2)}) async-start(), calls=%async_computation.9 | async-start | bytes 1114112
  394.0 227.3 %copy-start.4 = (bf16[256,512]{1,0:T(8,128)(2,1)S(1)}, bf16[256,512]{1,0:T(8,128)(2,1)}, u32[]{:S(2)}) copy-start(bf16[256,512]{1,0:T(8,128)(2,1)} %reduce-scatter.8.cloned.1.call-done) | copy-start | bytes 786436
  396.7 222.9 %all-reduce.2.cloned.1.call-start = ((), (), s32[]{:S(2)}) async-start(), calls=%async_computation.7 | async-start | bytes 524288 | tf_op jit(solution)/shard_map/psum | solution.py:65
  461.6 204.5 %all-gather.8.cloned.1.call-start = ((), (), s32[]{:S(2)}) async-start(), calls=%async_computation.8 | async-start | bytes 1114112 | tf_op jit(solution)/shard_map/all_gather | solution.py:66
Sparse Core Ops, SparseCore 0:
  10.4 43.9 all-gather.3
  104.4 95.0 reduce-scatter.5
  202.5 73.7 all-gather.5
  326.7 67.2 reduce-scatter.7
  396.9 62.9 reduce-scatter.9
  463.0 156.5 all-reduce.1
  622.0 44.0 all-gather.7
where the time goes:
time: 676 us; the launch traced here: 675 us
  waiting for transfers between devices  544 us (80%)
  other arithmetic  53.3 us (8%)
  local copies, waits for them, and re-layouts  43.5 us (6%)
  matrix products  18.9 us (3%)
  between operations  14.9 us (2%)
    psum x1, waiting for transfers between devices, shards(): weight_part = lax.psum(weight_part, 'col')  158 us
    reduce_scatter x1, waiting for transfers between devices, shards(): lax.psum_scatter(forward_terms.astype(jnp.bfloat16), 'col', scatter_dimen...  95.2 us
    all_gather x1, waiting for transfers between devices, shards(): upstream = lax.all_gather(own_upstream, 'col', axis=0, tiled=True)  74.7 us
    reduce_scatter x1, waiting for transfers between devices, shards(): lax.psum_scatter(backward_terms.astype(jnp.bfloat16), 'row', scatter_dime...  67.3 us
    unnamed x8, waiting for transfers between devices  63.3 us
    all_gather x1, waiting for transfers between devices, shards(): grad_weight = lax.all_gather(weight_part, 'row', axis=0, tiled=True)  43.7 us
    all_gather x1, waiting for transfers between devices, shards(): panel = lax.all_gather(projected, 'row', axis=0, tiled=True)  42.2 us
    scatter-add x2, other arithmetic, one_group(): return running.at[target_ids].add(products * alive_mask[:, None, None])  37.4 us
  transfers between devices with their start and end apart: 7, of which 7 were waited for; matrix products, arithmetic and copies ran while one was open for 0% of the time, Pallas kernels for 0%

commit v1 on v0

--- a/solution.py
+++ b/solution.py
@@ -33,6 +33,10 @@
 
 
 def shards(features, weight, entry_values, block_rows, block_cols, entry_counts, cotangent):
+
+    def scenes_fix(array_here, axis_key):
+        return jnp.sum(lax.all_gather(array_here, axis_name=axis_key), axis=0)
+
     values = entry_values[0, 0]
     row_ids = block_rows[0, 0]
     col_ids = block_cols[0, 0]
@@ -62,7 +66,7 @@
         features, grad_projected, (((0,), (0,)), ((), ())), preferred_element_type=jnp.float32
     )
     weight_part = lax.psum_scatter(weight_term, "row", scatter_dimension=0, tiled=True)
-    weight_part = lax.psum(weight_part, "col")
+    weight_part = scenes_fix(weight_part, "col")
     grad_weight = lax.all_gather(weight_part, "row", axis=0, tiled=True)
     grad_features = lax.dot_general(
         grad_projected, weight, (((1,), (1,)), ((), ())), preferred_element_type=jnp.float32

time: 676 us -> 562 us (0.83)
  waiting for transfers between devices: 544 us -> 431 us
    psum x1 -> x0, waiting for transfers between devices: 158 us -> none  [shards(): weight_part = lax.psum(weight_part, 'col')]
    reduce_scatter x0 -> x1, waiting for transfers between devices: none -> 63.2 us  [shards(): lax.psum_scatter(weight_term, 'row', scatter_dimension=0, tiled=True)]
    unnamed x8 -> x7, waiting for transfers between devices: 63.3 us -> 0.11 us
    all_gather x0 -> x1, waiting for transfers between devices: none -> 55.4 us  [scenes_fix(): return jnp.sum(lax.all_gather(array_here, axis_name=axis_key), axis=0)]
    all_gather x1, waiting for transfers between devices: 43.7 us -> 33.2 us  [shards(): grad_weight = lax.all_gather(weight_part, 'row', axis=0, tiled=True)]
  transfers between devices with their start and end apart: 7 -> 7, of which waited for: 7 -> 7; matrix products, arithmetic and copies ran while one was open for 0% -> 1% of each run, Pallas kernels for 0% -> 0%
where the time goes in v1:
time: 562 us; the launch traced here: 561 us
  waiting for transfers between devices  431 us (77%)
  other arithmetic  55.3 us (10%)
  local copies, waits for them, and re-layouts  40.2 us (7%)
  matrix products  18.9 us (3%)
  between operations  14.9 us (3%)
    reduce_scatter x1, waiting for transfers between devices, shards(): lax.psum_scatter(forward_terms.astype(jnp.bfloat16), 'col', scatter_dimen...  95.2 us
    all_gather x1, waiting for transfers between devices, shards(): upstream = lax.all_gather(own_upstream, 'col', axis=0, tiled=True)  74.7 us
    reduce_scatter x1, waiting for transfers between devices, shards(): lax.psum_scatter(backward_terms.astype(jnp.bfloat16), 'row', scatter_dime...  67.3 us
    reduce_scatter x1, waiting for transfers between devices, shards(): lax.psum_scatter(weight_term, 'row', scatter_dimension=0, tiled=True)  63.2 us
    all_gather x1, waiting for transfers between devices, scenes_fix(): return jnp.sum(lax.all_gather(array_here, axis_name=axis_key), axis=0)  55.4 us
    all_gather x1, waiting for transfers between devices, shards(): panel = lax.all_gather(projected, 'row', axis=0, tiled=True)  42.2 us
    scatter-add x2, other arithmetic, one_group(): return running.at[target_ids].add(products * alive_mask[:, None, None])  37.4 us
    all_gather x1, waiting for transfers between devices, shards(): grad_weight = lax.all_gather(weight_part, 'row', axis=0, tiled=True)  33.2 us
  transfers between devices with their start and end apart: 7, of which 7 were waited for; matrix products, arithmetic and copies ran while one was open for 1% of the time, Pallas kernels for 0%

profile of v1, /device:TPU:1, one launch (start us, length us, event | category | flops | bytes accessed | tf_op | source)
XLA Modules:
  0.0 560.7 jit_solution(14323665707563569961)
XLA Ops:
  7.2 2.2 convolution_convert_fusion.1
  12.1 42.2 %all-gather.6.cloned.1.call-done = bf16[4096,512]{1,0:T(8,128)(2,1)} async-done(((bf16[256,512]{1,0:T(8,128)(2,1)}), bf16[4096,512]{1,0:T(8,128)(2,1)}) %all-gather.6.cloned.1.call-update) | async-done | bytes 4194320 | tf_op jit(solution)/shard_map/all_gather | solution.py:49
  54.4 4.9 gather_fusion
  59.3 7.1 %multiply_bitcast_fusion.1 = f32[32,128,512]{1,2,0:T(8,128)} fusion(f32[32]{0:T(128)S(1)} %get-tuple-element.39, bf16[32,128,512]{2,1,0:T(8,128)(2,1)} %gather_fusion, pred[32]{0:T(512)(128)(4,1)S(1)} %get-tuple-element.38, bf16[1,1,32,128,128]{4,3,2,1,0:T(8,128)(2,1)S(1)} %copy-done), kind=kOutput, calls=%fused_computation.5 | convolution fusion | flops 541065216 | bytes 13631648 | tf_op jit(solution)/shard_map/while/body/eval_jaxpr/kab,kbf->kaf/dot_general | solution.py:20
  66.5 9.0 %copy.18 = f32[32,128,512]{2,1,0:T(8,128)} copy(f32[32,128,512]{1,2,0:T(8,128)} %multiply_bitcast_fusion.1) | data formatting | bytes 16777216 | tf_op jit(solution)/shard_map/while/body/eval_jaxpr/mul | solution.py:22
  75.5 4.3 broadcast.55.clone
  79.8 18.5 %scatter_fusion = f32[32,128,512]{2,1,0:T(8,128)} fusion(f32[32,128,512]{2,1,0:T(8,128)} %broadcast.55.clone, s32[32]{0:T(128)S(1)} %fusion.22, f32[32,128,512]{2,1,0:T(8,128)} %copy.18), kind=kCustom, calls=%fused_computation.2 | custom fusion | flops 2097152 | bytes 25165952 | tf_op jit(solution)/shard_map/while/body/eval_jaxpr/scatter-add | solution.py:22
  98.3 6.0 %convert_element_type.42 = bf16[32,128,512]{2,1,0:T(8,128)(2,1)} convert(f32[32,128,512]{2,1,0:T(8,128)} %scatter_fusion) | non-fusion elementwise | flops 2097152 | bytes 12582912 | tf_op jit(solution)/shard_map/convert_element_type | solution.py:54
  104.3 95.2 %reduce-scatter.6.cloned.1.call-done = bf16[256,512]{1,0:T(8,128)(2,1)} async-done(((bf16[4096,512]{1,0:T(8,128)(2,1)}), bf16[256,512]{1,0:T(8,128)(2,1)}) %reduce-scatter.6.cloned.1.call-update) | async-done | bytes 262160 | tf_op jit(solution)/shard_map/reduce_scatter | solution.py:53
  199.5 2.0 fusion.21
  201.6 74.7 %all-gather.8.cloned.1.call-done = bf16[4096,512]{1,0:T(8,128)(2,1)} async-done(((bf16[256,512]{1,0:T(8,128)(2,1)}), bf16[4096,512]{1,0:T(8,128)(2,1)}) %all-gather.8.cloned.1.call-update) | async-done | bytes 4194320 | tf_op jit(solution)/shard_map/all_gather | solution.py:58
  276.3 4.9 gather_fusion.1
  281.2 7.1 %multiply_bitcast_fusion = f32[32,128,512]{1,2,0:T(8,128)} fusion(f32[32]{0:T(128)S(1)} %get-tuple-element.39, bf16[32,128,512]{2,1,0:T(8,128)(2,1)} %gather_fusion.1, pred[32]{0:T(512)(128)(4,1)S(1)} %compare_and_fusion, bf16[1,1,32,128,128]{4,3,2,1,0:T(8,128)(2,1)S(1)} %copy-done), kind=kOutput, calls=%fused_computation.4 | convolution fusion | flops 541065216 | bytes 13631648 | tf_op jit(solution)/shard_map/while/body/eval_jaxpr/kba,kbf->kaf/dot_general | solution.py:18
  288.4 9.0 %copy.20 = f32[32,128,512]{2,1,0:T(8,128)} copy(f32[32,128,512]{1,2,0:T(8,128)} %multiply_bitcast_fusion) | data formatting | bytes 16777216 | tf_op jit(solution)/shard_map/while/body/eval_jaxpr/mul | solution.py:22
  297.4 4.3 broadcast.55
  301.7 18.9 %scatter_fusion.1 = f32[32,128,512]{2,1,0:T(8,128)} fusion(f32[32,128,512]{2,1,0:T(8,128)} %broadcast.55, s32[32]{0:T(128)S(1)} %fusion.23, f32[32,128,512]{2,1,0:T(8,128)} %copy.20), kind=kCustom, calls=%fused_computation.3 | custom fusion | flops 2097152 | bytes 25165952 | tf_op jit(solution)/shard_map/while/body/eval_jaxpr/scatter-add | solution.py:22
  320.6 6.0 %convert_element_type.48 = bf16[32,128,512]{2,1,0:T(8,128)(2,1)} convert(f32[32,128,512]{2,1,0:T(8,128)} %scatter_fusion.1) | non-fusion elementwise | flops 2097152 | bytes 12582912 | tf_op jit(solution)/shard_map/convert_element_type | solution.py:63
  326.7 67.3 %reduce-scatter.8.cloned.1.call-done = bf16[256,512]{1,0:T(8,128)(2,1)} async-done(((bf16[4096,512]{1,0:T(8,128)(2,1)}), bf16[256,512]{1,0:T(8,128)(2,1)}) %reduce-scatter.8.cloned.1.call-update) | async-done | bytes 262160 | tf_op jit(solution)/shard_map/reduce_scatter | solution.py:62
  394.0 1.3 convolution_bitcast_fusion
  396.7 63.2 %reduce-scatter.10.cloned.1.call-done = f32[32,512]{1,0:T(8,128)} async-done(((f32[512,512]{1,0:T(8,128)}), f32[32,512]{1,0:T(8,128)}) %reduce-scatter.10.cloned.1.call-update) | async-done | bytes 65552 | tf_op jit(solution)/shard_map/reduce_scatter | solution.py:68
  460.0 55.4 %all-gather.12.cloned.1.call-done = f32[512,512]{1,0:T(8,128)} async-done(((f32[32,512]{1,0:T(8,128)}), f32[512,512]{1,0:T(8,128)}) %all-gather.12.cloned.1.call-update) | async-done | bytes 1048592 | tf_op jit(solution)/shard_map/all_gather | solution.py:38
  515.4 1.9 reduce_sum.9
  518.4 33.2 %all-gather.10.cloned.1.call-done = f32[512,512]{1,0:T(8,128)} async-done(((f32[32,512]{1,0:T(8,128)}), f32[512,512]{1,0:T(8,128)}) %all-gather.10.cloned.1.call-update) | async-done | bytes 1048592 | tf_op jit(solution)/shard_map/all_gather | solution.py:70
  551.6 2.3 copy.31
  (40 shorter events, 4.8 us)
Async XLA Ops:
  7.2 52.2 %copy-start = (bf16[1,1,32,128,128]{4,3,2,1,0:T(8,128)(2,1)S(1)}, bf16[1,1,32,128,128]{4,3,2,1,0:T(8,128)(2,1)}, u32[]{:S(2)}) copy-start(bf16[1,1,32,128,128]{4,3,2,1,0:T(8,128)(2,1)} %param.11) | copy-start | bytes 3145732
  7.2 47.2 %all-gather.6.cloned.1.call-start = ((), (), s32[]{:S(2)}) async-start(), calls=%async_computation.3 | async-start | bytes 4456448 | tf_op jit(solution)/shard_map/all_gather | solution.py:49
  9.5 190.0 %reduce-scatter.6.cloned.1.call-start = ((), (), s32[]{:S(2)}) async-start(), calls=%async_computation.4 | async-start | bytes 4456448 | tf_op jit(solution)/shard_map/reduce_scatter | solution.py:53
  104.2 95.2 %copy-start.5 = (bf16[256,512]{1,0:T(8,128)(2,1)S(1)}, bf16[256,512]{1,0:T(8,128)(2,1)}, u32[]{:S(2)}) copy-start(bf16[256,512]{1,0:T(8,128)(2,1)} %param.15) | copy-start | bytes 786436
  104.3 97.3 %copy-start.7 = (s32[1,1,32]{2,1,0:T(1,128)S(1)}, s32[1,1,32]{2,1,0:T(1,128)}, u32[]{:S(2)}) copy-start(s32[1,1,32]{2,1,0:T(1,128)} %param.12) | copy-start | bytes 388
  104.3 97.3 %copy-start.6 = (s32[1,1,32]{2,1,0:T(1,128)S(1)}, s32[1,1,32]{2,1,0:T(1,128)}, u32[]{:S(2)}) copy-start(s32[1,1,32]{2,1,0:T(1,128)} %param.13) | copy-start | bytes 388
  104.3 172.0 %all-gather.8.cloned.1.call-start = ((), (), s32[]{:S(2)}) async-start(), calls=%async_computation.5 | async-start | bytes 4456448 | tf_op jit(solution)/shard_map/all_gather | solution.py:58
  201.5 192.5 %reduce-scatter.8.cloned.1.call-start = ((), (), s32[]{:S(2)}) async-start(), calls=%async_computation.6 | async-start | bytes 4456448 | tf_op jit(solution)/shard_map/reduce_scatter | solution.py:62
  326.6 67.4 %copy-start.3 = (bf16[256,512]{1,0:T(8,128)(2,1)S(1)}, bf16[256,512]{1,0:T(8,128)(2,1)}, u32[]{:S(2)}) copy-start(bf16[256,512]{1,0:T(8,128)(2,1)} %param.9) | copy-start | bytes 786436
  326.6 190.7 %copy-start.2 = (bf16[512,512]{1,0:T(8,128)(2,1)S(1)}, bf16[512,512]{1,0:T(8,128)(2,1)}, u32[]{:S(2)}) copy-start(bf16[512,512]{1,0:T(8,128)(2,1)} %param.10) | copy-start | bytes 1572868
  326.6 227.2 %copy-start.1 = (bf16[1,1,32,128,128]{4,3,2,1,0:T(8,128)(2,1)S(1)}, bf16[1,1,32,128,128]{4,3,2,1,0:T(8,128)(2,1)}, u32[]{:S(2)}) copy-start(bf16[1,1,32,128,128]{4,3,2,1,0:T(8,128)(2,1)} %param.11) | copy-start | bytes 3145732
  326.6 133.3 %reduce-scatter.10.cloned.1.call-start = ((), (), s32[]{:S(2)}) async-start(), calls=%async_computation.9 | async-start | bytes 1114112 | tf_op jit(solution)/shard_map/reduce_scatter | solution.py:68
  394.0 123.3 %copy-start.4 = (bf16[256,512]{1,0:T(8,128)(2,1)S(1)}, bf16[256,512]{1,0:T(8,128)(2,1)}, u32[]{:S(2)}) copy-start(bf16[256,512]{1,0:T(8,128)(2,1)} %reduce-scatter.8.cloned.1.call-done) | copy-start | bytes 786436
  396.7 118.7 %all-gather.12.cloned.1.call-start = ((), (), s32[]{:S(2)}) async-start(), calls=%async_computation.8 | async-start | bytes 1114112 | tf_op jit(solution)/shard_map/all_gather | solution.py:38
  460.0 91.6 %all-gather.10.cloned.1.call-start = ((), (), s32[]{:S(2)}) async-start(), calls=%async_computation.7 | async-start | bytes 1114112 | tf_op jit(solution)/shard_map/all_gather | solution.py:70
Sparse Core Ops, SparseCore 0:
  10.4 43.9 all-gather.5
  104.4 95.0 reduce-scatter.5
  202.5 73.7 all-gather.7
  326.7 67.2 reduce-scatter.7
  396.9 62.9 reduce-scatter.9
  462.2 53.1 all-gather.11
  517.8 33.7 all-gather.9
